TPU v7x, 256 devices: a whole 4x4x8 slice. The times are simulated.
256 devices in a mesh: lat: 8 (over y, z_lo), lon: 8 (over x, core), dp: 4 (over z_hi).
Axes of the slice: x: 4, y: 4, z: 8 (z_hi: 4, z_lo: 2; z = z_hi * 2 + z_lo), core: 2. Of those that a mesh axis runs over, the one named last changes fastest.
Arguments:
- state_grid: bfloat16 [4, 384, 768, 128], P('dp', ('lat', 'lon')), may hold values from -6 to 6
- cotangent: bfloat16 [4, 384, 768, 128], P('dp', ('lat', 'lon')), may hold values from -6 to 6
- legendre: bfloat16 [384, 384, 384], P(('lat', 'lon')), may hold values from -0.3125 to 0.3125
- wave_ids: int32 [384], replicated, may hold values from 0 to 383, each once
- weights: bfloat16 [384, 2, 4, 1024], P('lat'), may hold values from -0.75 to 0.75
Outputs:
- input_grad: bfloat16 [4, 384, 768, 128], P('dp', ('lat', 'lon'))
- weight_grad: float32 [384, 2, 4, 1024], P('lat')
Inputs may be any that keep to these rules, and one draw needn't show every extreme that they name: wave_ids[j] is the wavenumber of slot j; each of 0 to 383 stands in exactly one slot.
All inputs are finite; a program needn't handle non-finite values.
Results may differ from a plain program's by a relative error of at most 0.034.
Values may be sent and summed in bfloat16 or wider, within the bound.
No kernel may reach another device: no remote copies, remote signals or barrier semaphores. Data moves between devices by JAX's collectives and lax.ppermute only.
A program may use at most 128 MiB of HBM per device.

v0:
```python
import math
import jax
import jax.numpy as jnp
from jax import lax
from jax.sharding import PartitionSpec as P

NLON = 768
GROUPS = 4
GROUP_WIDTH = 32


def build_tables(wave_ids):
    columns = jnp.arange(NLON, dtype=jnp.int32)
    phase_int = wave_ids[:, None] * columns[None, :] % NLON
    angles = phase_int.astype(jnp.float32) * jnp.float32(2.0 * math.pi / NLON)
    factor = jnp.float32(1.0 / math.sqrt(NLON))
    paired = jnp.stack([jnp.cos(angles) * factor, -jnp.sin(angles) * factor], axis=1)
    forward_table = paired.reshape(2 * wave_ids.shape[0], NLON)
    doubling = jnp.where(wave_ids == 0, 1.0, 2.0).astype(jnp.float32)
    inverse_table = forward_table * jnp.repeat(doubling, 2)[:, None]
    return (forward_table.astype(jnp.bfloat16), inverse_table.astype(jnp.bfloat16))


def build_kernel(weights):
    degree_count = weights.shape[0]
    real_part = weights[:, 0].reshape(degree_count, GROUPS, GROUP_WIDTH, GROUP_WIDTH)
    imag_part = weights[:, 1].reshape(degree_count, GROUPS, GROUP_WIDTH, GROUP_WIDTH)
    upper_rows = jnp.stack([real_part, imag_part], axis=3)
    lower_rows = jnp.stack([-imag_part, real_part], axis=3)
    return jnp.stack([upper_rows, lower_rows], axis=2)


def gelu_slope(branch):
    normal_cdf = 0.5 * (1.0 + lax.erf(branch * (1.0 / math.sqrt(2.0))))
    density = jnp.exp(-0.5 * branch * branch) * (1.0 / math.sqrt(2.0 * math.pi))
    return normal_cdf + branch * density


def shards(state_grid, cotangent, legendre, wave_ids, weights):
    lat_count = lax.axis_size("lat")
    lon_count = lax.axis_size("lon")
    samples, rows_dev, lon_cells, channels = state_grid.shape
    slot_count, lat_cells, degree_count = legendre.shape
    slot_reals = 2 * slot_count
    first_slot = (lax.axis_index("lat") * lon_count + lax.axis_index("lon")) * slot_count
    held_waves = lax.dynamic_slice_in_dim(wave_ids, first_slot, slot_count)
    degree_ids = jnp.arange(degree_count, dtype=jnp.int32)
    masked = jnp.where(
        degree_ids[None, None, :] >= held_waves[:, None, None],
        legendre,
        jnp.zeros((), legendre.dtype),
    )
    slot_order = wave_ids.reshape(lat_count, lon_count, slot_count).transpose(1, 0, 2).reshape(-1)
    forward_table, inverse_table = build_tables(slot_order)
    kernel = build_kernel(weights)

    def analyze(source, twiddle):
        spectra = jnp.einsum(
            "srnc,kn->srkc", source, twiddle, preferred_element_type=jnp.float32
        ).astype(jnp.bfloat16)
        gathered = lax.all_to_all(
            lax.all_to_all(spectra, "lon", split_axis=2, concat_axis=1, tiled=True),
            "lat",
            split_axis=2,
            concat_axis=1,
            tiled=True,
        )
        blocks = gathered.reshape(samples, lat_cells, slot_count, 2 * channels)
        spectral = jnp.einsum("samc,mal->slmc", blocks, masked, preferred_element_type=jnp.float32)
        spectral = spectral.astype(jnp.bfloat16).reshape(
            samples, degree_count, slot_reals, channels
        )
        return lax.all_to_all(spectral, "lat", split_axis=1, concat_axis=2, tiled=True)

    def synthesize(spectral, twiddle):
        joined = lax.all_to_all(spectral, "lat", split_axis=2, concat_axis=1, tiled=True)
        blocks = joined.reshape(samples, degree_count, slot_count, 2 * channels)
        spectra = jnp.einsum(
            "slmc,mal->samc", blocks, masked, preferred_element_type=jnp.float32
        ).astype(jnp.bfloat16)
        spectra = spectra.reshape(samples, lat_cells, slot_reals, channels)
        pencil = lax.all_to_all(
            lax.all_to_all(spectra, "lat", split_axis=1, concat_axis=2, tiled=True),
            "lon",
            split_axis=1,
            concat_axis=2,
            tiled=True,
        )
        return jnp.einsum("srkc,kn->srnc", pencil, twiddle, preferred_element_type=jnp.float32)

    def split_groups(spectral):
        return spectral.reshape(samples, spectral.shape[1], -1, 2, GROUPS, GROUP_WIDTH)

    coef_fwd = analyze(state_grid, forward_table)
    coef_six = split_groups(coef_fwd)
    mixed_coef = jnp.einsum(
        "slmpgi,lgpiqo->slmqgo", coef_six, kernel, preferred_element_type=jnp.float32
    ).astype(jnp.bfloat16)
    branch = synthesize(mixed_coef.reshape(coef_fwd.shape), inverse_table)
    pulled = (cotangent.astype(jnp.float32) * gelu_slope(branch)).astype(jnp.bfloat16)
    back_coef = analyze(pulled, inverse_table)
    back_six = split_groups(back_coef)
    outer_sums = jnp.einsum(
        "slmpgi,slmqgo->lgpiqo", coef_six, back_six, preferred_element_type=jnp.float32
    )
    real_grad = outer_sums[:, :, 0, :, 0, :] + outer_sums[:, :, 1, :, 1, :]
    imag_grad = outer_sums[:, :, 0, :, 1, :] - outer_sums[:, :, 1, :, 0, :]
    local_grad = jnp.stack([real_grad, imag_grad], axis=1).reshape(weights.shape)
    weight_grad = lax.psum(local_grad.astype(jnp.bfloat16), ("lon", "dp")).astype(jnp.float32)
    demixed = jnp.einsum(
        "slmqgo,lgpiqo->slmpgi", back_six, kernel, preferred_element_type=jnp.float32
    ).astype(jnp.bfloat16)
    returned = synthesize(demixed.reshape(back_coef.shape), forward_table)
    input_grad = (cotangent.astype(jnp.float32) + returned).astype(jnp.bfloat16)
    return (input_grad, weight_grad)


def solution(mesh):
    return jax.shard_map(
        shards,
        mesh=mesh,
        in_specs=(
            P("dp", ("lat", "lon"), None, None),
            P("dp", ("lat", "lon"), None, None),
            P(("lat", "lon"), None, None),
            P(),
            P("lat", None, None, None),
        ),
        out_specs=(P("dp", ("lat", "lon"), None, None), P("lat", None, None, None)),
        check_vma=False,
    )
```

profile of v0, /device:TPU:8, one launch (start us, length us, event | category | flops | bytes accessed | tf_op | source)
XLA Modules:
  0.0 725.3 jit_solution(13457028617643623277)
XLA Ops:
  8.2 4.9 cosine_multiply_fusion
  15.6 3.7 reshape.366
  22.5 25.9 %all_to_all.192 = bf16[1,6,768,128]{3,1,0,2:T(8,128)(2,1)S(1)} all-to-all(bf16[1,6,768,128]{3,1,0,2:T(8,128)(2,1)S(1)} %copy.223), channel_id=1, replica_groups=mesh['lat'=8,'lon'=8,'dp'=4] {'lon'}, dimensions={2} | all-to-all | bytes 2359296 | tf_op jit(solution)/shard_map/all_to_all | solution.py:62
  50.1 6.5 all-to-all-start.1
  57.4 13.8 %all-to-all-done.1 = bf16[1,48,96,128]{3,1,0,2:T(8,128)(2,1)S(1)} async-done(((bf16[1,48,96,128]{3,1,0,2:T(8,128)(2,1)}), bf16[1,48,96,128]{3,1,0,2:T(8,128)(2,1)S(1)}, u32[]{:S(2)}, u32[]{:S(2)}) %all-to-all-start.1) | async-done | bytes 1179680 | tf_op jit(solution)/shard_map/all_to_all | solution.py:61
  71.2 3.0 copy.280
  74.2 4.4 reshape.378
  78.7 3.4 convolution_convert_fusion.1
  82.1 2.9 copy.229
  85.0 6.4 all-to-all-start.2
  100.2 3.0 pad_maximum_fusion
  103.2 12.7 %copy.232 = bf16[48,4,2,32,2,32]{3,5,2,4,1,0:T(8,128)(2,1)} copy(bf16[48,4,2,32,2,32]{0,5,4,3,1,2:T(8,128)(2,1)} %pad_maximum_fusion) | data formatting | bytes 3145728 | tf_op jit(solution)/shard_map/stack | solution.py:30
  120.3 8.3 %copy.270 = bf16[48,48,2,4,32,1]{1,4,2,5,3,0:T(8,128)(2,1)} copy(bf16[48,48,2,4,32,1]{0,4,3,2,1,5:T(8,128)(2,1)} %bitcast.179) | data formatting | bytes 2359296 | tf_op jit(solution)/shard_map/reshape.8
  128.5 6.7 fusion
  135.3 8.3 %copy.234 = bf16[1,48,48,2,4,32]{1,5,4,3,2,0:T(8,128)(2,1)} copy(bf16[1,48,48,2,4,32]{2,5,3,4,1,0:T(8,128)(2,1)} %fusion) | data formatting | bytes 2359296 | tf_op jit(solution)/shard_map/convert_element_type | solution.py:98
  143.5 3.2 copy.235
  146.7 19.4 %all_to_all.193 = bf16[1,48,96,128]{3,1,0,2:T(8,128)(2,1)} all-to-all(bf16[1,48,96,128]{3,1,0,2:T(8,128)(2,1)S(1)} %copy.235), channel_id=1, replica_groups=mesh['lat'=8,'lon'=8,'dp'=4] {'lat'}, dimensions={2} | all-to-all | bytes 2359296 | tf_op jit(solution)/shard_map/all_to_all | solution.py:76
  166.2 4.2 copy.283
  170.4 4.4 reshape.379
  174.8 3.5 convolution_convert_fusion.3
  178.3 2.9 copy.238
  181.2 21.5 %all_to_all.194 = bf16[1,384,12,128]{3,2,0,1:T(8,128)(2,1)S(1)} all-to-all(bf16[1,384,12,128]{3,2,0,1:T(8,128)(2,1)} %copy.238), channel_id=1, replica_groups=mesh['lat'=8,'lon'=8,'dp'=4] {'lat'}, dimensions={1} | all-to-all | bytes 2359296 | tf_op jit(solution)/shard_map/all_to_all | solution.py:83
  204.4 4.3 all-to-all-start.5
  211.1 14.9 %all-to-all-done.5 = bf16[1,48,96,128]{3,2,0,1:T(8,128)(2,1)} async-done(((bf16[1,48,96,128]{3,2,0,1:T(8,128)(2,1)}), bf16[1,48,96,128]{3,2,0,1:T(8,128)(2,1)}, u32[]{:S(2)}, u32[]{:S(2)}) %all-to-all-start.5) | async-done | bytes 1179680 | tf_op jit(solution)/shard_map/all_to_all | solution.py:82
  227.4 4.8 fusion.15
  234.4 24.2 %all_to_all.195 = bf16[1,6,768,128]{3,1,0,2:T(8,128)(2,1)S(1)} all-to-all(bf16[1,6,768,128]{3,1,0,2:T(8,128)(2,1)S(1)} %copy.244), channel_id=1, replica_groups=mesh['lat'=8,'lon'=8,'dp'=4] {'lon'}, dimensions={2} | all-to-all | bytes 2359296 | tf_op jit(solution)/shard_map/all_to_all | solution.py:62
  259.3 20.1 %all_to_all.196 = bf16[1,48,96,128]{3,1,0,2:T(8,128)(2,1)S(1)} all-to-all(bf16[1,48,96,128]{3,1,0,2:T(8,128)(2,1)S(1)} %copy.247), channel_id=1, replica_groups=mesh['lat'=8,'lon'=8,'dp'=4] {'lat'}, dimensions={2} | all-to-all | bytes 2359296 | tf_op jit(solution)/shard_map/all_to_all | solution.py:61
  279.4 3.0 copy.284
  282.4 4.4 reshape.380
  291.1 5.1 all-to-all-start.8
  296.3 11.6 %copy.253 = bf16[48,4,2,32,2,32]{5,3,4,2,1,0:T(8,128)(2,1)} copy(bf16[48,4,2,32,2,32]{0,5,4,3,1,2:T(8,128)(2,1)} %pad_maximum_fusion) | data formatting | bytes 3145728 | tf_op jit(solution)/shard_map/stack | solution.py:30
  307.8 6.3 all-to-all-done.8
  314.5 2.7 copy.252
  317.2 8.3 %copy.273 = bf16[48,48,2,4,32,1]{1,4,2,5,3,0:T(8,128)(2,1)} copy(bf16[48,48,2,4,32,1]{0,4,3,2,1,5:T(8,128)(2,1)} %bitcast.182) | data formatting | bytes 2359296 | tf_op jit(solution)/shard_map/reshape.39
  325.5 6.8 fusion.1
  332.3 8.3 %copy.255 = bf16[1,48,48,2,4,32]{1,5,4,3,2,0:T(8,128)(2,1)} copy(bf16[1,48,48,2,4,32]{2,5,3,4,1,0:T(8,128)(2,1)} %fusion.1) | data formatting | bytes 2359296 | tf_op jit(solution)/shard_map/convert_element_type | solution.py:112
  340.6 3.2 copy.256
  343.8 19.7 %all_to_all.197 = bf16[1,48,96,128]{3,1,0,2:T(8,128)(2,1)S(1)} all-to-all(bf16[1,48,96,128]{3,1,0,2:T(8,128)(2,1)S(1)} %copy.256), channel_id=1, replica_groups=mesh['lat'=8,'lon'=8,'dp'=4] {'lat'}, dimensions={2} | all-to-all | bytes 2359296 | tf_op jit(solution)/shard_map/all_to_all | solution.py:76
  363.5 3.0 copy.287
  366.4 4.4 reshape.381
  375.3 5.3 all-to-all-start.10
  380.6 8.3 %copy.276 = bf16[48,48,2,4,32,1]{1,4,5,2,3,0:T(8,128)(2,1)} copy(bf16[48,48,2,4,32,1]{0,4,3,2,1,5:T(8,128)(2,1)} %bitcast.180) | data formatting | bytes 2359296 | tf_op jit(solution)/shard_map/reshape.8
  388.9 12.5 %fusion.41 = f32[48,4,2,32,2,32]{5,3,4,2,1,0:T(8,128)} fusion(bf16[48,48,2,4,32,1]{1,4,5,2,3,0:T(8,128)(2,1)} %copy.276, bf16[48,48,2,4,32,1]{1,4,2,5,3,0:T(8,128)(2,1)} %copy.273), kind=kOutput, calls=%fused_computation.66 | convolution fusion | flops 75497472 | bytes 5505024 | tf_op jit(solution)/shard_map/slmpgi,slmqgo->lgpiqo/dot_general | solution.py:103
  403.1 4.3 all-to-all-start.11
  407.4 7.5 %fusion.3 = (bf16[48,4,1,32,1,32]{5,3,4,2,1,0:T(8,128)(2,1)}, bf16[48,4,1,32,1,32]{5,3,4,2,1,0:T(8,128)(2,1)S(1)}) fusion(f32[48,4,2,32,2,32]{5,3,4,2,1,0:T(8,128)} %fusion.41), kind=kLoop, calls=%fused_computation.9 | loop fusion | flops 786432 | bytes 3932160 | tf_op jit(solution)/shard_map/convert.3
  415.0 2.9 reshape.382
  421.6 290.0 %all-reduce.2.cloned.1.call-done = bf16[48,2,4,1024]{3,0,2,1:T(8,128)(2,1)} async-done(((bf16[48,2,4,1024]{3,0,2,1:T(8,128)(2,1)}), bf16[48,2,4,1024]{3,0,2,1:T(8,128)(2,1)}) %all-reduce.2.cloned.1.call-update) | async-done | bytes 786448 | tf_op jit(solution)/shard_map/psum | solution.py:109
  711.6 2.9 copy.269
  (62 shorter events, 48.9 us)
Async XLA Ops:
  7.2 12.2 %copy-start = (bf16[1,6,768,128]{3,2,1,0:T(8,128)(2,1)S(1)}, bf16[1,6,768,128]{3,2,1,0:T(8,128)(2,1)}, u32[]{:S(2)}) copy-start(bf16[1,6,768,128]{3,2,1,0:T(8,128)(2,1)} %param.5) | copy-start | bytes 3538948
  50.1 21.1 %all-to-all-start.1 = ((bf16[1,48,96,128]{3,1,0,2:T(8,128)(2,1)}), bf16[1,48,96,128]{3,1,0,2:T(8,128)(2,1)S(1)}, u32[]{:S(2)}, u32[]{:S(2)}) async-start(bf16[1,48,96,128]{3,1,0,2:T(8,128)(2,1)} %copy.226), calls=%async_computation.1 | async-start | bytes 2359296 | tf_op jit(solution)/shard_map/all_to_all | solution.py:61
  85.0 6.4 copy-start.3
  85.0 30.9 %all-to-all-start.2 = ((bf16[1,384,12,128]{3,2,0,1:T(8,128)(2,1)}), bf16[1,384,12,128]{3,2,0,1:T(8,128)(2,1)}, u32[]{:S(2)}, u32[]{:S(2)}) async-start(bf16[1,384,12,128]{3,2,0,1:T(8,128)(2,1)} %copy.229), calls=%async_computation.2 | async-start | bytes 3145728 | tf_op jit(solution)/shard_map/all_to_all | solution.py:73
  204.4 21.6 %all-to-all-start.5 = ((bf16[1,48,96,128]{3,2,0,1:T(8,128)(2,1)}), bf16[1,48,96,128]{3,2,0,1:T(8,128)(2,1)}, u32[]{:S(2)}, u32[]{:S(2)}) async-start(bf16[1,48,96,128]{3,2,0,1:T(8,128)(2,1)} %copy.241), calls=%async_computation.5 | async-start | bytes 2359296 | tf_op jit(solution)/shard_map/all_to_all | solution.py:82
  291.1 23.0 %all-to-all-start.8 = ((bf16[1,384,12,128]{3,2,0,1:T(8,128)(2,1)}), bf16[1,384,12,128]{3,2,0,1:T(8,128)(2,1)S(1)}, u32[]{:S(2)}, u32[]{:S(2)}) async-start(bf16[1,384,12,128]{3,2,0,1:T(8,128)(2,1)} %copy.250), calls=%async_computation.8 | async-start | bytes 3145728 | tf_op jit(solution)/shard_map/all_to_all | solution.py:73
  375.3 26.1 %all-to-all-start.10 = ((bf16[1,384,12,128]{3,2,0,1:T(8,128)(2,1)}), bf16[1,384,12,128]{3,2,0,1:T(8,128)(2,1)S(1)}, u32[]{:S(2)}, u32[]{:S(2)}) async-start(bf16[1,384,12,128]{3,2,0,1:T(8,128)(2,1)} %copy.259), calls=%async_computation.10 | async-start | bytes 3145728 | tf_op jit(solution)/shard_map/all_to_all | solution.py:83
  403.1 311.3 %all-to-all-start.11 = ((bf16[1,48,96,128]{3,2,0,1:T(8,128)(2,1)}), bf16[1,48,96,128]{3,2,0,1:T(8,128)(2,1)}, u32[]{:S(2)}, u32[]{:S(2)}) async-start(bf16[1,48,96,128]{3,2,0,1:T(8,128)(2,1)} %copy.262), calls=%async_computation.11 | async-start | bytes 2359296 | tf_op jit(solution)/shard_map/all_to_all | solution.py:82
  407.4 304.2 %all-reduce.2.cloned.1.call-start = ((), (), s32[]{:S(2)}) async-start(), calls=%async_computation.12 | async-start | bytes 1572864 | tf_op jit(solution)/shard_map/psum | solution.py:109
  419.5 1.6 copy-start.2
  714.5 1.6 copy-start.4
  716.1 2.1 copy-start.1
Sparse Core Ops, SparseCore 0:
  420.8 290.7 all-reduce.1
where the time goes:
time: 735 us; the launch traced here: 725 us
  waiting for transfers between devices  325 us (44%)
  local copies, waits for them, and re-layouts  155 us (21%)
  blocking collectives  131 us (18%)
  matrix products  47 us (6%)
  starting transfers between devices  31.8 us (4%)
  other arithmetic  20.7 us (3%)
  between operations  14.6 us (2%)
    psum x1, waiting for transfers between devices, shards(): lax.psum(local_grad.astype(jnp.bfloat16), ('lon', 'dp')).astype(jnp.float32)  290 us
    another operation x11, local copies, waits for them, and re-layouts  55.7 us
    all_to_all x2, blocking collectives, analyze(): lax.all_to_all(spectra, 'lon', split_axis=2, concat_axis=1, tiled=True)  50.1 us
    all_to_all x2, blocking collectives, synthesize(): lax.all_to_all(spectral, 'lat', split_axis=2, concat_axis=1, tiled=True)  39.1 us
    another operation x2, local copies, waits for them, and re-layouts, build_kernel(): return jnp.stack([upper_rows, lower_rows], axis=2)  24.2 us
    all_to_all x1, blocking collectives, synthesize(): lax.all_to_all(spectra, 'lat', split_axis=1, concat_axis=2, tiled=True)  21.5 us
    all_to_all x1, blocking collectives, analyze(): lax.all_to_all(lax.all_to_all(spectra, 'lon', split_axis=2, concat_axis=1...  20.1 us
    all_to_all x2, waiting for transfers between devices, synthesize(): lax.all_to_all(lax.all_to_all(spectra, 'lat', split_axis=1, concat_axis=2...  14.9 us
  transfers between devices with their start and end apart: 7, of which 4 were waited for; matrix products, arithmetic and copies ran while one was open for 11% of the time, Pallas kernels for 0%

commit v1 on v0

--- a/solution.py
+++ b/solution.py
@@ -106,7 +106,9 @@
     real_grad = outer_sums[:, :, 0, :, 0, :] + outer_sums[:, :, 1, :, 1, :]
     imag_grad = outer_sums[:, :, 0, :, 1, :] - outer_sums[:, :, 1, :, 0, :]
     local_grad = jnp.stack([real_grad, imag_grad], axis=1).reshape(weights.shape)
-    weight_grad = lax.psum(local_grad.astype(jnp.bfloat16), ("lon", "dp")).astype(jnp.float32)
+    weight_grad = lax.psum(lax.psum(local_grad.astype(jnp.bfloat16), "dp"), "lon").astype(
+        jnp.float32
+    )
     demixed = jnp.einsum(
         "slmqgo,lgpiqo->slmpgi", back_six, kernel, preferred_element_type=jnp.float32
     ).astype(jnp.bfloat16)

time: 735 us -> 558 us (0.76)
  waiting for transfers between devices: 325 us -> 157 us
    psum x1 -> x2, waiting for transfers between devices: 290 us -> 122 us  [the longest x1 66.9 us: shards(): lax.psum(lax.psum(local_grad.astype(jnp.bfloat16), 'dp'), 'lon')]
  transfers between devices with their start and end apart: 7 -> 8, of which waited for: 4 -> 5; matrix products, arithmetic and copies ran while one was open for 11% -> 13% of each run, Pallas kernels for 0% -> 0%
where the time goes in v1:
time: 558 us; the launch traced here: 548 us
  waiting for transfers between devices  157 us (28%)
  local copies, waits for them, and re-layouts  156 us (28%)
  blocking collectives  131 us (23%)
  matrix products  42.4 us (8%)
  starting transfers between devices  31.2 us (6%)
  other arithmetic  16.4 us (3%)
  between operations  14.6 us (3%)
    psum x1, waiting for transfers between devices, shards(): lax.psum(lax.psum(local_grad.astype(jnp.bfloat16), 'dp'), 'lon')  66.9 us
    another operation x11, local copies, waits for them, and re-layouts  55.6 us
    psum x1, waiting for transfers between devices, shards(): lax.psum(local_grad.astype(jnp.bfloat16), 'dp')  55 us
    all_to_all x2, blocking collectives, analyze(): lax.all_to_all(spectra, 'lon', split_axis=2, concat_axis=1, tiled=True)  50.1 us
    all_to_all x2, blocking collectives, synthesize(): lax.all_to_all(spectral, 'lat', split_axis=2, concat_axis=1, tiled=True)  39.1 us
    another operation x2, local copies, waits for them, and re-layouts, build_kernel(): return jnp.stack([upper_rows, lower_rows], axis=2)  24.2 us
    all_to_all x1, blocking collectives, synthesize(): lax.all_to_all(spectra, 'lat', split_axis=1, concat_axis=2, tiled=True)  21.5 us
    all_to_all x1, blocking collectives, analyze(): lax.all_to_all(lax.all_to_all(spectra, 'lon', split_axis=2, concat_axis=1...  20.1 us
  transfers between devices with their start and end apart: 8, of which 5 were waited for; matrix products, arithmetic and copies ran while one was open for 13% of the time, Pallas kernels for 0%

profile of v1, /device:TPU:8, one launch (start us, length us, event | category | flops | bytes accessed | tf_op | source)
XLA Modules:
  0.0 548.2 jit_solution(1825001330478332372)
XLA Ops:
  8.2 4.9 cosine_multiply_fusion
  15.6 3.7 reshape.366
  22.5 25.9 %all_to_all.192 = bf16[1,6,768,128]{3,1,0,2:T(8,128)(2,1)S(1)} all-to-all(bf16[1,6,768,128]{3,1,0,2:T(8,128)(2,1)S(1)} %copy.223), channel_id=1, replica_groups=mesh['lat'=8,'lon'=8,'dp'=4] {'lon'}, dimensions={2} | all-to-all | bytes 2359296 | tf_op jit(solution)/shard_map/all_to_all | solution.py:62
  50.1 6.5 %all-to-all-start.1 = ((bf16[1,48,96,128]{3,1,0,2:T(8,128)(2,1)}), bf16[1,48,96,128]{3,1,0,2:T(8,128)(2,1)S(1)}, u32[]{:S(2)}, u32[]{:S(2)}) async-start(bf16[1,48,96,128]{3,1,0,2:T(8,128)(2,1)} %copy.226), calls=%async_computation.1 | async-start | bytes 2359296 | tf_op jit(solution)/shard_map/all_to_all | solution.py:61
  57.4 13.8 %all-to-all-done.1 = bf16[1,48,96,128]{3,1,0,2:T(8,128)(2,1)S(1)} async-done(((bf16[1,48,96,128]{3,1,0,2:T(8,128)(2,1)}), bf16[1,48,96,128]{3,1,0,2:T(8,128)(2,1)S(1)}, u32[]{:S(2)}, u32[]{:S(2)}) %all-to-all-start.1) | async-done | bytes 1179680 | tf_op jit(solution)/shard_map/all_to_all | solution.py:61
  71.2 3.0 copy.280
  74.2 4.4 reshape.378
  78.7 3.4 convolution_convert_fusion.1
  82.1 2.9 copy.229
  85.0 6.4 %all-to-all-start.2 = ((bf16[1,384,12,128]{3,2,0,1:T(8,128)(2,1)}), bf16[1,384,12,128]{3,2,0,1:T(8,128)(2,1)}, u32[]{:S(2)}, u32[]{:S(2)}) async-start(bf16[1,384,12,128]{3,2,0,1:T(8,128)(2,1)} %copy.229), calls=%async_computation.2 | async-start | bytes 3145728 | tf_op jit(solution)/shard_map/all_to_all | solution.py:73
  100.2 3.0 pad_maximum_fusion
  103.2 12.7 %copy.232 = bf16[48,4,2,32,2,32]{3,5,2,4,1,0:T(8,128)(2,1)} copy(bf16[48,4,2,32,2,32]{0,5,4,3,1,2:T(8,128)(2,1)} %pad_maximum_fusion) | data formatting | bytes 3145728 | tf_op jit(solution)/shard_map/stack | solution.py:30
  120.3 8.3 %copy.270 = bf16[48,48,2,4,32,1]{1,4,2,5,3,0:T(8,128)(2,1)} copy(bf16[48,48,2,4,32,1]{0,4,3,2,1,5:T(8,128)(2,1)} %bitcast.179) | data formatting | bytes 2359296 | tf_op jit(solution)/shard_map/reshape.8
  128.5 6.7 %fusion = bf16[1,48,48,2,4,32]{2,5,3,4,1,0:T(8,128)(2,1)} fusion(bf16[48,4,2,32,2,32]{3,5,2,4,1,0:T(8,128)(2,1)} %copy.232, bf16[48,48,2,4,32,1]{1,4,2,5,3,0:T(8,128)(2,1)} %copy.270), kind=kOutput, calls=%fused_computation.4 | convolution fusion | flops 76087296 | bytes 3932160 | tf_op jit(solution)/shard_map/slmpgi,lgpiqo->slmqgo/dot_general | solution.py:96
  135.3 8.3 %copy.234 = bf16[1,48,48,2,4,32]{1,5,4,3,2,0:T(8,128)(2,1)} copy(bf16[1,48,48,2,4,32]{2,5,3,4,1,0:T(8,128)(2,1)} %fusion) | data formatting | bytes 2359296 | tf_op jit(solution)/shard_map/convert_element_type | solution.py:98
  143.5 3.2 copy.235
  146.7 19.4 %all_to_all.193 = bf16[1,48,96,128]{3,1,0,2:T(8,128)(2,1)} all-to-all(bf16[1,48,96,128]{3,1,0,2:T(8,128)(2,1)S(1)} %copy.235), channel_id=1, replica_groups=mesh['lat'=8,'lon'=8,'dp'=4] {'lat'}, dimensions={2} | all-to-all | bytes 2359296 | tf_op jit(solution)/shard_map/all_to_all | solution.py:76
  166.2 4.2 copy.283
  170.4 4.4 reshape.379
  174.8 3.5 convolution_convert_fusion.3
  178.3 2.9 copy.238
  181.2 21.5 %all_to_all.194 = bf16[1,384,12,128]{3,2,0,1:T(8,128)(2,1)S(1)} all-to-all(bf16[1,384,12,128]{3,2,0,1:T(8,128)(2,1)} %copy.238), channel_id=1, replica_groups=mesh['lat'=8,'lon'=8,'dp'=4] {'lat'}, dimensions={1} | all-to-all | bytes 2359296 | tf_op jit(solution)/shard_map/all_to_all | solution.py:83
  204.4 4.3 all-to-all-start.5
  211.1 14.9 %all-to-all-done.5 = bf16[1,48,96,128]{3,2,0,1:T(8,128)(2,1)} async-done(((bf16[1,48,96,128]{3,2,0,1:T(8,128)(2,1)}), bf16[1,48,96,128]{3,2,0,1:T(8,128)(2,1)}, u32[]{:S(2)}, u32[]{:S(2)}) %all-to-all-start.5) | async-done | bytes 1179680 | tf_op jit(solution)/shard_map/all_to_all | solution.py:82
  227.4 4.8 fusion.15
  234.4 24.2 %all_to_all.195 = bf16[1,6,768,128]{3,1,0,2:T(8,128)(2,1)S(1)} all-to-all(bf16[1,6,768,128]{3,1,0,2:T(8,128)(2,1)S(1)} %copy.244), channel_id=1, replica_groups=mesh['lat'=8,'lon'=8,'dp'=4] {'lon'}, dimensions={2} | all-to-all | bytes 2359296 | tf_op jit(solution)/shard_map/all_to_all | solution.py:62
  259.3 20.1 %all_to_all.196 = bf16[1,48,96,128]{3,1,0,2:T(8,128)(2,1)S(1)} all-to-all(bf16[1,48,96,128]{3,1,0,2:T(8,128)(2,1)S(1)} %copy.247), channel_id=1, replica_groups=mesh['lat'=8,'lon'=8,'dp'=4] {'lat'}, dimensions={2} | all-to-all | bytes 2359296 | tf_op jit(solution)/shard_map/all_to_all | solution.py:61
  279.4 3.0 copy.284
  282.4 4.4 reshape.380
  291.1 5.1 all-to-all-start.8
  296.3 11.6 %copy.253 = bf16[48,4,2,32,2,32]{5,3,4,2,1,0:T(8,128)(2,1)} copy(bf16[48,4,2,32,2,32]{0,5,4,3,1,2:T(8,128)(2,1)} %pad_maximum_fusion) | data formatting | bytes 3145728 | tf_op jit(solution)/shard_map/stack | solution.py:30
  307.8 6.3 %all-to-all-done.8 = bf16[1,384,12,128]{3,2,0,1:T(8,128)(2,1)S(1)} async-done(((bf16[1,384,12,128]{3,2,0,1:T(8,128)(2,1)}), bf16[1,384,12,128]{3,2,0,1:T(8,128)(2,1)S(1)}, u32[]{:S(2)}, u32[]{:S(2)}) %all-to-all-start.8) | async-done | bytes 1179680 | tf_op jit(solution)/shard_map/all_to_all | solution.py:73
  317.2 8.2 %copy.273 = bf16[48,48,2,4,32,1]{1,4,2,5,3,0:T(8,128)(2,1)} copy(bf16[48,48,2,4,32,1]{0,4,3,2,1,5:T(8,128)(2,1)} %bitcast.182) | data formatting | bytes 2359296 | tf_op jit(solution)/shard_map/reshape.39
  325.5 6.7 %fusion.1 = bf16[1,48,48,2,4,32]{2,5,3,4,1,0:T(8,128)(2,1)} fusion(bf16[48,4,2,32,2,32]{5,3,4,2,1,0:T(8,128)(2,1)} %copy.253, bf16[48,48,2,4,32,1]{1,4,2,5,3,0:T(8,128)(2,1)} %copy.273), kind=kOutput, calls=%fused_computation.5 | convolution fusion | flops 76087296 | bytes 3932160 | tf_op jit(solution)/shard_map/slmqgo,lgpiqo->slmpgi/dot_general | solution.py:112
  332.2 8.3 %copy.255 = bf16[1,48,48,2,4,32]{1,5,4,3,2,0:T(8,128)(2,1)} copy(bf16[1,48,48,2,4,32]{2,5,3,4,1,0:T(8,128)(2,1)} %fusion.1) | data formatting | bytes 2359296 | tf_op jit(solution)/shard_map/convert_element_type | solution.py:114
  340.4 3.2 copy.256
  343.6 19.7 %all_to_all.197 = bf16[1,48,96,128]{3,1,0,2:T(8,128)(2,1)S(1)} all-to-all(bf16[1,48,96,128]{3,1,0,2:T(8,128)(2,1)S(1)} %copy.256), channel_id=1, replica_groups=mesh['lat'=8,'lon'=8,'dp'=4] {'lat'}, dimensions={2} | all-to-all | bytes 2359296 | tf_op jit(solution)/shard_map/all_to_all | solution.py:76
  363.3 3.0 copy.287
  366.3 4.4 reshape.381
  375.2 5.1 all-to-all-start.10
  380.5 8.3 %copy.276 = bf16[48,48,2,4,32,1]{1,4,5,2,3,0:T(8,128)(2,1)} copy(bf16[48,48,2,4,32,1]{0,4,3,2,1,5:T(8,128)(2,1)} %bitcast.180) | data formatting | bytes 2359296 | tf_op jit(solution)/shard_map/reshape.8
  388.7 8.0 %fusion.41 = f32[48,4,2,32,2,32]{5,3,4,2,1,0:T(8,128)S(1)} fusion(bf16[48,48,2,4,32,1]{1,4,5,2,3,0:T(8,128)(2,1)} %copy.276, bf16[48,48,2,4,32,1]{1,4,2,5,3,0:T(8,128)(2,1)} %copy.273), kind=kOutput, calls=%fused_computation.66 | convolution fusion | flops 75497472 | bytes 5505024 | tf_op jit(solution)/shard_map/slmpgi,slmqgo->lgpiqo/dot_general | solution.py:103
  396.7 3.2 fusion.3
  402.9 2.9 reshape.383
  408.7 3.7 all-to-all-start.11
  412.4 55.0 %all-reduce.3.cloned.1.call-done = bf16[48,2,4,1024]{3,0,2,1:T(8,128)(2,1)} async-done(((bf16[48,2,4,1024]{3,0,2,1:T(8,128)(2,1)}), bf16[48,2,4,1024]{3,0,2,1:T(8,128)(2,1)}) %all-reduce.3.cloned.1.call-update) | async-done | bytes 786448 | tf_op jit(solution)/shard_map/psum | solution.py:109
  467.9 66.9 %all-reduce.5.cloned.1.call-done = bf16[48,2,4,1024]{3,0,2,1:T(8,128)(2,1)} async-done(((bf16[48,2,4,1024]{3,0,2,1:T(8,128)(2,1)}), bf16[48,2,4,1024]{3,0,2,1:T(8,128)(2,1)}) %all-reduce.5.cloned.1.call-update) | async-done | bytes 786448 | tf_op jit(solution)/shard_map/psum | solution.py:109
  534.9 2.9 copy.269
  (65 shorter events, 52.4 us)
Async XLA Ops:
  7.2 12.2 %copy-start = (bf16[1,6,768,128]{3,2,1,0:T(8,128)(2,1)S(1)}, bf16[1,6,768,128]{3,2,1,0:T(8,128)(2,1)}, u32[]{:S(2)}) copy-start(bf16[1,6,768,128]{3,2,1,0:T(8,128)(2,1)} %param.5) | copy-start | bytes 3538948
  50.1 21.1 %all-to-all-start.1 = ((bf16[1,48,96,128]{3,1,0,2:T(8,128)(2,1)}), bf16[1,48,96,128]{3,1,0,2:T(8,128)(2,1)S(1)}, u32[]{:S(2)}, u32[]{:S(2)}) async-start(bf16[1,48,96,128]{3,1,0,2:T(8,128)(2,1)} %copy.226), calls=%async_computation.1 | async-start | bytes 2359296 | tf_op jit(solution)/shard_map/all_to_all | solution.py:61
  85.0 6.4 %copy-start.3 = (bf16[48,2,4,1024]{3,2,1,0:T(4,128)(2,1)S(1)}, bf16[48,2,4,1024]{3,2,1,0:T(4,128)(2,1)}, u32[]{:S(2)}) copy-start(bf16[48,2,4,1024]{3,2,1,0:T(4,128)(2,1)} %param.9) | copy-start | bytes 2359300
  85.0 30.9 %all-to-all-start.2 = ((bf16[1,384,12,128]{3,2,0,1:T(8,128)(2,1)}), bf16[1,384,12,128]{3,2,0,1:T(8,128)(2,1)}, u32[]{:S(2)}, u32[]{:S(2)}) async-start(bf16[1,384,12,128]{3,2,0,1:T(8,128)(2,1)} %copy.229), calls=%async_computation.2 | async-start | bytes 3145728 | tf_op jit(solution)/shard_map/all_to_all | solution.py:73
  204.4 21.6 %all-to-all-start.5 = ((bf16[1,48,96,128]{3,2,0,1:T(8,128)(2,1)}), bf16[1,48,96,128]{3,2,0,1:T(8,128)(2,1)}, u32[]{:S(2)}, u32[]{:S(2)}) async-start(bf16[1,48,96,128]{3,2,0,1:T(8,128)(2,1)} %copy.241), calls=%async_computation.5 | async-start | bytes 2359296 | tf_op jit(solution)/shard_map/all_to_all | solution.py:82
  291.1 23.0 %all-to-all-start.8 = ((bf16[1,384,12,128]{3,2,0,1:T(8,128)(2,1)}), bf16[1,384,12,128]{3,2,0,1:T(8,128)(2,1)S(1)}, u32[]{:S(2)}, u32[]{:S(2)}) async-start(bf16[1,384,12,128]{3,2,0,1:T(8,128)(2,1)} %copy.250), calls=%async_computation.8 | async-start | bytes 3145728 | tf_op jit(solution)/shard_map/all_to_all | solution.py:73
  375.2 31.8 %all-to-all-start.10 = ((bf16[1,384,12,128]{3,2,0,1:T(8,128)(2,1)}), bf16[1,384,12,128]{3,2,0,1:T(8,128)(2,1)S(1)}, u32[]{:S(2)}, u32[]{:S(2)}) async-start(bf16[1,384,12,128]{3,2,0,1:T(8,128)(2,1)} %copy.259), calls=%async_computation.10 | async-start | bytes 3145728 | tf_op jit(solution)/shard_map/all_to_all | solution.py:83
  380.3 87.1 %all-reduce.3.cloned.1.call-start = ((), (), s32[]{:S(2)}) async-start(), calls=%async_computation.12 | async-start | bytes 1572864 | tf_op jit(solution)/shard_map/psum | solution.py:109
  408.7 58.7 %copy-start.2 = (bf16[384,2,768]{2,1,0:T(2,128)(2,1)S(1)}, bf16[384,2,768]{2,1,0:T(2,128)(2,1)}, u32[]{:S(2)}) copy-start(bf16[384,2,768]{2,1,0:T(2,128)(2,1)} %copy.215) | copy-start | bytes 3538948
  408.7 129.1 %all-to-all-start.11 = ((bf16[1,48,96,128]{3,2,0,1:T(8,128)(2,1)}), bf16[1,48,96,128]{3,2,0,1:T(8,128)(2,1)S(1)}, u32[]{:S(2)}, u32[]{:S(2)}) async-start(bf16[1,48,96,128]{3,2,0,1:T(8,128)(2,1)} %copy.262), calls=%async_computation.11 | async-start | bytes 2359296 | tf_op jit(solution)/shard_map/all_to_all | solution.py:82
  412.4 122.5 %all-reduce.5.cloned.1.call-start = ((), (), s32[]{:S(2)}) async-start(), calls=%async_computation.13 | async-start | bytes 1572864 | tf_op jit(solution)/shard_map/psum | solution.py:109
  537.7 1.3 copy-start.4
  539.0 2.2 copy-start.1
Sparse Core Ops, SparseCore 0:
  407.0 60.3 all-reduce.2
  469.8 65.0 all-reduce.4
